TPU v7x, 32 devices: a whole 2x2x4 slice. The times are simulated.
32 devices in a mesh: req: 4 (over x, core), head: 8 (over z, y).
Axes of the slice: x: 2, y: 2, z: 4, core: 2. Of those that a mesh axis runs over, the one named last changes fastest.
Arguments:
- stretch_acts: bfloat16 [8, 256, 2048], P(None, ('req', 'head')), may hold values from -6 to 6
- cache_prefill: bfloat16 [8, 8, 256, 32, 128], P('req', None, 'head'), may hold values from -600 to 600
- stretch_lens: int32 [8], replicated, may hold values from 1 to 256, 1280 in all
- prefix_lens: int32 [8], replicated, may hold values from 1 to 256, 1280 in all
- req_order: int32 [8], replicated, may hold values from 0 to 7, each once
- attn_gain: bfloat16 [2048], replicated, may hold values from 0.25 to 1.75
- in_weight: bfloat16 [2048, 32, 192], P(None, 'head'), may hold values from -0.125 to 0.125
- slopes: float32 [32], P('head'), may hold values from 0.00390625 to 0.5
- out_weight: bfloat16 [32, 64, 2048], P('head'), may hold values from -0.125 to 0.125
- mlp_gain: bfloat16 [2048], replicated, may hold values from 0.25 to 1.75
- up_weight: bfloat16 [2048, 8192], P(None, 'head'), may hold values from -0.125 to 0.125
- down_weight: bfloat16 [8192, 2048], P('head'), may hold values from -0.0625 to 0.0625
Outputs:
- layer_out: bfloat16 [8, 256, 2048], P(None, ('req', 'head'))
- cache_decode: bfloat16 [8, 8, 256, 32, 128], P(None, 'req', None, 'head')
Inputs may be any that keep to these rules, and one draw needn't show every extreme that they name: `stretch_lens`: the entries sum to 1280 and the largest is exactly 256. `prefix_lens`: the entries sum to 1280 and the largest is exactly 256. `req_order`: each request appears once.
All inputs are finite; a program needn't handle non-finite values.
Results may differ from a plain program's by a relative error of at most 0.013.
The roundings to bfloat16 on the way count: a program that leaves them out, or rounds other values in their place, can miss the bound.
Values may be sent and summed in bfloat16 or wider, within the bound.
No kernel may reach another device: no remote copies, remote signals or barrier semaphores. Data moves between devices by JAX's collectives and lax.ppermute only.
A program may use at most 128 MiB of HBM per device.

v0:
```python
import math
import jax
import jax.numpy as jnp
from jax import lax
from jax.sharding import PartitionSpec as P

EPSILON = 1e-05


def layer_norm(values, gain):
    average = jnp.mean(values, axis=-1, keepdims=True)
    centred = values - average
    variance = jnp.mean(centred * centred, axis=-1, keepdims=True)
    return centred * lax.rsqrt(variance + EPSILON) * gain.astype(jnp.float32)


def attend(queries, pairs, prefix_len, slopes, head_dim):
    stretch = queries.shape[0]
    prefix = pairs.shape[0] - stretch
    keys_part = pairs[..., :head_dim]
    values_part = pairs[..., head_dim:]
    scores = jnp.einsum("qhd,khd->hqk", queries, keys_part, preferred_element_type=jnp.float32) * (
        1.0 / math.sqrt(head_dim)
    )
    row_index = jnp.arange(stretch, dtype=jnp.int32)
    key_index = jnp.arange(prefix + stretch, dtype=jnp.int32)
    in_prefix = key_index < prefix
    query_pos = prefix_len + row_index
    key_pos = jnp.where(in_prefix, key_index, prefix_len + key_index - prefix)
    allowed = jnp.where(
        in_prefix[None, :],
        key_index[None, :] < prefix_len,
        (key_index - prefix)[None, :] <= row_index[:, None],
    )
    distance = (query_pos[:, None] - key_pos[None, :]).astype(jnp.float32)
    scores = scores - slopes[:, None, None] * distance[None]
    scores = jnp.where(allowed[None], scores, -jnp.inf)
    highest = jnp.max(scores, axis=-1, keepdims=True)
    expo = jnp.exp(scores - highest)
    soft = (expo / jnp.sum(expo, axis=-1, keepdims=True)).astype(jnp.bfloat16)
    context = jnp.einsum("hqk,khd->qhd", soft, values_part, preferred_element_type=jnp.float32)
    return context.astype(jnp.bfloat16).reshape(stretch, -1)


def local(
    stretch_acts,
    cache_prefill,
    stretch_lens,
    prefix_lens,
    req_order,
    attn_gain,
    in_weight,
    slopes,
    out_weight,
    mlp_gain,
    up_weight,
    down_weight,
):
    req_count = lax.axis_size("req")
    head_count = lax.axis_size("head")
    req_index = lax.axis_index("req")
    head_index = lax.axis_index("head")
    requests = stretch_acts.shape[0]
    stretch_rows = stretch_acts.shape[1]
    features = stretch_acts.shape[2]
    group_size = requests // req_count
    span_rows = head_count * stretch_rows
    stretch_max = req_count * span_rows
    prefix_rows = cache_prefill.shape[2]
    heads_here = in_weight.shape[1]
    pair_width = cache_prefill.shape[4]
    head_dim = pair_width // 2
    members = lax.dynamic_slice_in_dim(req_order, req_index * group_size, group_size)
    member_stretch = jnp.take(stretch_lens, members)
    member_prefix = jnp.take(prefix_lens, members)
    ordered_prefix = jnp.take(prefix_lens, req_order)
    positions = head_index * prefix_rows + jnp.arange(prefix_rows, dtype=jnp.int32)
    keep = positions[None, :] < ordered_prefix[:, None]
    local_layers = cache_prefill.shape[0]
    halves = []
    for layer in range(local_layers):
        dealt_cache = jnp.where(
            keep[None, :, :, None, None],
            jnp.take(cache_prefill[layer : layer + 1], req_order, axis=1),
            jnp.zeros((), cache_prefill.dtype),
        )
        halves.append(
            lax.all_to_all(
                lax.all_to_all(dealt_cache, "head", split_axis=3, concat_axis=2, tiled=True),
                "req",
                split_axis=1,
                concat_axis=0,
                tiled=True,
            )
        )
    current = halves[0][0]
    relaid = jnp.stack(halves, axis=1).reshape((req_count * local_layers,) + halves[0].shape[1:])
    dealt_acts = jnp.take(stretch_acts, req_order, axis=0)
    dealt_rows = lax.all_to_all(dealt_acts, "req", split_axis=0, concat_axis=1, tiled=True).reshape(
        group_size, req_count, stretch_rows, features
    )
    gathered = lax.all_gather(dealt_rows, "head", axis=2, tiled=True)
    normed = (
        layer_norm(gathered.astype(jnp.float32), attn_gain)
        .astype(jnp.bfloat16)
        .reshape(group_size * stretch_max, features)
    )
    mixed = jnp.dot(
        normed,
        in_weight.reshape(features, heads_here * 3 * head_dim),
        preferred_element_type=jnp.float32,
    )
    mixed = mixed.reshape(group_size, stretch_max, heads_here, 3 * head_dim).astype(jnp.bfloat16)
    contexts = []
    for member in range(group_size):
        pairs = jnp.concatenate([current[member], mixed[member, :, :, head_dim:]], axis=0)
        contexts.append(
            attend(mixed[member, :, :, :head_dim], pairs, member_prefix[member], slopes, head_dim)
        )
    context = jnp.concatenate(contexts, axis=0)
    partial_attn = jnp.dot(
        context,
        out_weight.reshape(heads_here * head_dim, features),
        preferred_element_type=jnp.float32,
    )
    partial_attn = partial_attn.reshape(group_size, req_count, span_rows, features)
    attn_rows = lax.psum_scatter(
        partial_attn.astype(jnp.bfloat16), "head", scatter_dimension=2, tiled=True
    ).astype(jnp.float32)
    residual_rows = dealt_rows.astype(jnp.float32) + attn_rows
    normed_rows = layer_norm(residual_rows, mlp_gain).astype(jnp.bfloat16)
    normed_all = lax.all_gather(normed_rows, "head", axis=2, tiled=True)
    inner = jax.nn.gelu(
        jnp.dot(
            normed_all.reshape(group_size * stretch_max, features),
            up_weight,
            preferred_element_type=jnp.float32,
        ),
        approximate=False,
    ).astype(jnp.bfloat16)
    partial_mlp = jnp.dot(inner, down_weight, preferred_element_type=jnp.float32).reshape(
        group_size, req_count, span_rows, features
    )
    mlp_rows = lax.psum_scatter(
        partial_mlp.astype(jnp.bfloat16), "head", scatter_dimension=2, tiled=True
    ).astype(jnp.float32)
    row_number = (
        jnp.arange(req_count, dtype=jnp.int32)[:, None] * head_count + head_index
    ) * stretch_rows + jnp.arange(stretch_rows, dtype=jnp.int32)[None, :]
    usable = row_number[None] < member_stretch[:, None, None]
    result = jnp.where(
        usable[..., None], residual_rows + mlp_rows, jnp.zeros((), jnp.float32)
    ).astype(jnp.bfloat16)
    returned = lax.all_to_all(result, "req", split_axis=1, concat_axis=0, tiled=True).reshape(
        requests, stretch_rows, features
    )
    inverse = jnp.argsort(req_order)
    layer_out = jnp.take(returned, inverse, axis=0)
    return (layer_out, relaid)


def solution(mesh):
    return jax.shard_map(
        local,
        mesh=mesh,
        in_specs=(
            P(None, ("req", "head"), None),
            P("req", None, "head", None, None),
            P(),
            P(),
            P(),
            P(),
            P(None, "head", None),
            P("head"),
            P("head", None, None),
            P(),
            P(None, "head"),
            P("head", None),
        ),
        out_specs=(P(None, ("req", "head"), None), P(None, "req", None, "head", None)),
        check_vma=False,
    )
```

profile of v0, /device:TPU:0, one launch (start us, length us, event | category | flops | bytes accessed | tf_op | source)
XLA Modules:
  0.0 427.9 jit_solution(1506799252785771041)
XLA Ops:
  7.2 0.8 compare_select_fusion.1
  8.0 1.4 gather_fusion
  10.1 1.5 gather_fusion.2
  12.4 4.2 all-to-all-start
  16.6 5.2 %slice_bitcast_fusion = (bf16[8,32,32,128]{3,2,1,0:T(8,128)(2,1)}, bf16[8,32,32,128]{3,2,1,0:T(8,128)(2,1)}) fusion(bf16[2,8,32,32,128]{4,3,2,1,0:T(8,128)(2,1)} %param.19), kind=kLoop, calls=%fused_computation.31 | loop fusion | bytes 8388608 | tf_op jit(solution)/shard_map/jit(_take)/Arg_0.9 | solution.py:84
  21.8 3.7 gather_fusion.6
  25.5 3.7 gather_fusion.3
  29.3 3.5 fusion.12
  32.8 2.1 copy.51
  35.6 6.5 %all-to-all-start.1 = ((bf16[1,8,32,32,128]{4,2,1,0,3:T(8,128)(2,1)}), bf16[1,8,32,32,128]{4,2,1,0,3:T(8,128)(2,1)}, u32[]{:S(2)}, u32[]{:S(2)}) async-start(bf16[1,8,32,32,128]{4,2,1,0,3:T(8,128)(2,1)} %copy.51), calls=%async_computation.1 | async-start | bytes 4194304 | tf_op jit(solution)/shard_map/all_to_all | solution.py:89
  45.6 1.3 iota_compare_fusion.1
  49.6 0.9 subtract_convert_fusion.1
  50.5 0.9 subtract_convert_fusion
  51.4 57.4 %all-to-all-done.1 = bf16[1,8,32,32,128]{4,2,1,0,3:T(8,128)(2,1)} async-done(((bf16[1,8,32,32,128]{4,2,1,0,3:T(8,128)(2,1)}), bf16[1,8,32,32,128]{4,2,1,0,3:T(8,128)(2,1)}, u32[]{:S(2)}, u32[]{:S(2)}) %all-to-all-start.1) | async-done | bytes 2097184 | tf_op jit(solution)/shard_map/all_to_all | solution.py:89
  108.8 2.0 copy.52
  110.9 1.9 copy.53
  112.8 4.5 %all-to-all-start.2 = ((bf16[1,8,256,4,128]{4,2,3,0,1:T(8,128)(2,1)}), bf16[1,8,256,4,128]{4,2,3,0,1:T(8,128)(2,1)}, u32[]{:S(2)}, u32[]{:S(2)}) async-start(bf16[1,8,256,4,128]{4,2,3,0,1:T(8,128)(2,1)} %bitcast.121), calls=%async_computation.2 | async-start | bytes 4194304 | tf_op jit(solution)/shard_map/all_to_all | solution.py:88
  117.5 2.1 convert_reduce_fusion
  121.3 1.8 fusion.21
  123.1 0.9 copy-done.12
  124.1 18.9 %all-to-all-done.2 = bf16[1,8,256,4,128]{4,2,3,0,1:T(8,128)(2,1)} async-done(((bf16[1,8,256,4,128]{4,2,3,0,1:T(8,128)(2,1)}), bf16[1,8,256,4,128]{4,2,3,0,1:T(8,128)(2,1)}, u32[]{:S(2)}, u32[]{:S(2)}) %all-to-all-start.2) | async-done | bytes 2097184 | tf_op jit(solution)/shard_map/all_to_all | solution.py:88
  143.0 2.9 copy.55
  146.6 2.2 fusion.122
  148.8 2.3 convolution_convert_fusion.3
  151.1 2.0 fusion.121
  153.1 2.4 convolution_convert_fusion.2
  156.4 2.9 copy.82
  159.3 4.5 %reshape.468 = bf16[64,16384]{1,0:T(8,128)(2,1)} reshape(bf16[64,2,4,2048]{3,2,1,0:T(4,128)(2,1)} %bitcast.123) | data formatting | bytes 4194304
  164.5 66.1 %reduce-scatter.7.cloned.1.call-done = bf16[8,16384]{1,0:T(8,128)(2,1)} async-done(((bf16[64,16384]{1,0:T(8,128)(2,1)}), bf16[8,16384]{1,0:T(8,128)(2,1)}) %reduce-scatter.7.cloned.1.call-update) | async-done | bytes 262160
  230.6 1.1 reshape.469
  232.4 0.9 multiply_convert_fusion
  233.3 2.1 copy.61
  235.5 3.6 all-to-all-start.4
  239.3 73.6 %all-gather.5.cloned.1.call-done = bf16[2,4,64,2048]{3,2,0,1:T(8,128)(2,1)} async-done(((bf16[2,4,8,2048]{3,2,0,1:T(8,128)(2,1)}), bf16[2,4,64,2048]{3,2,0,1:T(8,128)(2,1)}) %all-gather.5.cloned.1.call-update) | async-done | bytes 2097168 | tf_op jit(solution)/shard_map/all_gather | solution.py:132
  313.0 3.2 copy.59
  316.1 14.3 %convolution_convert_fusion = bf16[512,2048]{1,0:T(8,128)(2,1)} fusion(bf16[1024,2048]{1,0:T(8,128)(2,1)} %param.29, bf16[512,2048]{1,0:T(8,128)(2,1)} %bitcast.134, bf16[2048,1024]{1,0:T(8,128)(2,1)} %param.28), kind=kOutput, calls=%fused_computation.20 | convolution fusion | flops 4330094592 | bytes 12582912 | tf_op jit(solution)/shard_map/dot_general | solution.py:141
  330.4 4.5 %copy.81 = bf16[2,4,64,2048]{3,1,0,2:T(4,128)(2,1)} copy(bf16[2,4,64,2048]{3,2,1,0:T(8,128)(2,1)} %bitcast.135) | data formatting | bytes 4194304
  334.9 4.5 %reshape.470 = bf16[64,16384]{1,0:T(8,128)(2,1)} reshape(bf16[64,2,4,2048]{3,2,1,0:T(4,128)(2,1)} %bitcast.124) | data formatting | bytes 4194304
  339.4 1.0 sort.17
  340.8 1.9 copy.63
  342.7 3.6 all-to-all-start.5
  346.5 58.5 %reduce-scatter.9.cloned.1.call-done = bf16[8,16384]{1,0:T(8,128)(2,1)} async-done(((bf16[64,16384]{1,0:T(8,128)(2,1)}), bf16[8,16384]{1,0:T(8,128)(2,1)}) %reduce-scatter.9.cloned.1.call-update) | async-done | bytes 262160
  405.1 1.1 reshape.471
  406.2 1.0 select_convert_fusion
  407.2 3.7 all-to-all-start.3
  410.9 2.0 pad_maximum_fusion
  412.9 5.5 %copy.65 = bf16[4,2,2,256,4,128]{5,4,3,2,1,0:T(4,128)(2,1)} copy(bf16[4,2,2,256,4,128]{5,3,4,2,0,1:T(8,128)(2,1)S(1)} %pad_maximum_fusion) | data formatting | bytes 8388608 | tf_op jit(solution)/shard_map/stack | solution.py:97
  419.1 1.5 gather_fusion.5
  (93 shorter events, 15.7 us)
Async XLA Ops:
  7.2 114.1 %copy-start = (bf16[2048,4,192]{0,2,1:T(8,128)(2,1)S(1)}, bf16[2048,4,192]{0,2,1:T(8,128)(2,1)}, u32[]{:S(2)}) copy-start(bf16[2048,4,192]{0,2,1:T(8,128)(2,1)} %param.24) | copy-start | bytes 9437188
  12.4 22.5 %all-to-all-start = ((bf16[8,8,2048]{2,1,0:T(8,128)(2,1)}), bf16[8,8,2048]{2,1,0:T(8,128)(2,1)S(1)}, u32[]{:S(2)}, u32[]{:S(2)}) async-start(bf16[8,8,2048]{2,1,0:T(8,128)(2,1)} %broadcast_select_fusion.1), calls=%async_computation | async-start | bytes 524288 | tf_op jit(solution)/shard_map/all_to_all | solution.py:99
  34.9 8.0 %copy-start.17 = (s32[8]{0:T(128)S(1)}, s32[8]{0:T(128)}, u32[]{:S(2)}) copy-start(s32[8]{0:T(128)} %param.22) | copy-start | bytes 100
  34.9 8.1 %copy-start.2 = (s32[8]{0:T(128)S(1)}, s32[8]{0:T(128)}, u32[]{:S(2)}) copy-start(s32[8]{0:T(128)} %param.21) | copy-start | bytes 100
  34.9 8.7 %copy-start.3 = (s32[8]{0:T(128)S(1)}, s32[8]{0:T(128)}, u32[]{:S(2)}) copy-start(s32[8]{0:T(128)} %param.20) | copy-start | bytes 100
  34.9 9.3 %copy-start.15 = (bf16[2048]{0:T(1024)(128)(2,1)S(1)}, bf16[2048]{0:T(1024)(128)(2,1)}, u32[]{:S(2)}) copy-start(bf16[2048]{0:T(1024)(128)(2,1)} %param.23) | copy-start | bytes 12292
  34.9 0.7 copy-start.5
  35.6 73.2 %all-to-all-start.1 = ((bf16[1,8,32,32,128]{4,2,1,0,3:T(8,128)(2,1)}), bf16[1,8,32,32,128]{4,2,1,0,3:T(8,128)(2,1)}, u32[]{:S(2)}, u32[]{:S(2)}) async-start(bf16[1,8,32,32,128]{4,2,1,0,3:T(8,128)(2,1)} %copy.51), calls=%async_computation.1 | async-start | bytes 4194304 | tf_op jit(solution)/shard_map/all_to_all | solution.py:89
  42.1 75.4 %all-gather.3.cloned.1.call-start = ((), (), s32[]{:S(2)}) async-start(), calls=%async_computation.8 | async-start | bytes 2359296 | tf_op jit(solution)/shard_map/all_gather | solution.py:102
  112.8 30.2 %all-to-all-start.2 = ((bf16[1,8,256,4,128]{4,2,3,0,1:T(8,128)(2,1)}), bf16[1,8,256,4,128]{4,2,3,0,1:T(8,128)(2,1)}, u32[]{:S(2)}, u32[]{:S(2)}) async-start(bf16[1,8,256,4,128]{4,2,3,0,1:T(8,128)(2,1)} %bitcast.121), calls=%async_computation.2 | async-start | bytes 4194304 | tf_op jit(solution)/shard_map/all_to_all | solution.py:88
  117.2 113.3 %reduce-scatter.7.cloned.1.call-start = ((), (), s32[]{:S(2)}) async-start(), calls=%async_computation.10 | async-start | bytes 2359296
  117.5 2.2 copy-start.4
  123.1 0.9 copy-start.12
  124.0 22.6 %copy-start.11 = (f32[256,512]{1,0:T(8,128)S(1)}, f32[256,512]{1,0:T(8,128)}, u32[]{:S(2)}) copy-start(f32[256,512]{1,0:T(8,128)} %subtract_convert_fusion.1) | copy-start | bytes 1572868
  124.1 22.6 %copy-start.18 = (f32[4]{0:T(128)S(1)}, f32[4]{0:T(128)}, u32[]{:S(2)}) copy-start(f32[4]{0:T(128)} %param.25) | copy-start | bytes 52
  146.6 4.5 %copy-start.13 = (bf16[256,4,128]{0,2,1:T(8,128)(2,1)}, bf16[256,4,128]{0,2,1:T(8,128)(2,1)S(1)}, u32[]{:S(2)}) copy-start(bf16[256,4,128]{0,2,1:T(8,128)(2,1)S(1)} %get-tuple-element.12) | copy-start | bytes 786436
  146.6 2.2 copy-start.14
  148.8 2.3 copy-start.10
  153.1 2.5 copy-start.9
  163.8 0.7 copy-start.16
  163.8 68.0 %copy-start.6 = (bf16[8,8,2048]{2,1,0:T(8,128)(2,1)S(1)}, bf16[8,8,2048]{2,1,0:T(8,128)(2,1)}, u32[]{:S(2)}) copy-start(bf16[8,8,2048]{2,1,0:T(8,128)(2,1)} %copy-done.5) | copy-start | bytes 786436
  163.8 69.5 %copy-start.7 = (bf16[1,8,32,32,128]{4,3,2,1,0:T(8,128)(2,1)S(1)}, bf16[1,8,32,32,128]{4,3,2,1,0:T(8,128)(2,1)}, u32[]{:S(2)}) copy-start(bf16[1,8,32,32,128]{4,3,2,1,0:T(8,128)(2,1)} %get-tuple-element.17) | copy-start | bytes 6291460
  163.8 149.2 %all-gather.5.cloned.1.call-start = ((), (), s32[]{:S(2)}) async-start(), calls=%async_computation.9 | async-start | bytes 2359296 | tf_op jit(solution)/shard_map/all_gather | solution.py:132
  235.5 104.9 %all-to-all-start.4 = ((bf16[1,8,32,32,128]{4,2,1,0,3:T(8,128)(2,1)}), bf16[1,8,32,32,128]{4,2,1,0,3:T(8,128)(2,1)S(1)}, u32[]{:S(2)}, u32[]{:S(2)}) async-start(bf16[1,8,32,32,128]{4,2,1,0,3:T(8,128)(2,1)} %copy.61), calls=%async_computation.4 | async-start | bytes 4194304 | tf_op jit(solution)/shard_map/all_to_all | solution.py:89
  239.1 166.0 %reduce-scatter.9.cloned.1.call-start = ((), (), s32[]{:S(2)}) async-start(), calls=%async_computation.11 | async-start | bytes 2359296
  342.7 64.5 %all-to-all-start.5 = ((bf16[1,8,256,4,128]{4,2,3,0,1:T(8,128)(2,1)}), bf16[1,8,256,4,128]{4,2,3,0,1:T(8,128)(2,1)S(1)}, u32[]{:S(2)}, u32[]{:S(2)}) async-start(bf16[1,8,256,4,128]{4,2,3,0,1:T(8,128)(2,1)} %bitcast.44), calls=%async_computation.5 | async-start | bytes 4194304 | tf_op jit(solution)/shard_map/all_to_all | solution.py:88
  407.2 11.2 %all-to-all-start.3 = ((bf16[2,4,8,2048]{3,2,0,1:T(8,128)(2,1)}), bf16[2,4,8,2048]{3,2,0,1:T(8,128)(2,1)S(1)}, u32[]{:S(2)}, u32[]{:S(2)}) async-start(bf16[2,4,8,2048]{3,2,0,1:T(8,128)(2,1)} %select_convert_fusion), calls=%async_computation.3 | async-start | bytes 524288 | tf_op jit(solution)/shard_map/all_to_all | solution.py:154
  412.9 8.5 %copy-start.1 = (bf16[2048,4,192]{0,2,1:T(8,128)(2,1)S(1)}, bf16[2048,4,192]{0,2,1:T(8,128)(2,1)}, u32[]{:S(2)}) copy-start(bf16[2048,4,192]{0,2,1:T(8,128)(2,1)} %param.24) | copy-start | bytes 9437188
  418.4 0.7 copy-start.8
Sparse Core Ops, SparseCore 0:
  45.7 71.0 all-gather.2
  163.9 66.6 reduce-scatter.6
  233.4 79.4 all-gather.4
  339.5 65.4 reduce-scatter.8
where the time goes:
time: 429 us; the launch traced here: 428 us
  waiting for transfers between devices  275 us (64%)
  local copies, waits for them, and re-layouts  63.7 us (15%)
  starting transfers between devices  26.6 us (6%)
  matrix products  25.6 us (6%)
  other arithmetic  22.4 us (5%)
  between operations  14.2 us (3%)
    unnamed x6, waiting for transfers between devices  125 us
    all_gather x1, waiting for transfers between devices, local(): normed_all = lax.all_gather(normed_rows, 'head', axis=2, tiled=True)  73.6 us
    all_to_all x2, waiting for transfers between devices, local(): lax.all_to_all(dealt_cache, 'head', split_axis=3, concat_axis=2, tiled=True)  57.4 us
    unnamed x44, local copies, waits for them, and re-layouts  21.7 us
    all_to_all x2, waiting for transfers between devices, local(): lax.all_to_all(lax.all_to_all(dealt_cache, 'head', split_axis=3, concat_a...  18.9 us
    dot_general x1, matrix products, local(): jnp.dot(inner, down_weight, preferred_element_type=jnp.float32)  14.3 us
    all_to_all x2, starting transfers between devices, local(): lax.all_to_all(dealt_cache, 'head', split_axis=3, concat_axis=2, tiled=True)  10.1 us
  transfers between devices with their start and end apart: 10, of which 5 were waited for; matrix products, arithmetic and copies ran while one was open for 18% of the time, Pallas kernels for 0%

commit v1 on v0

--- a/solution.py
+++ b/solution.py
@@ -5,6 +5,18 @@
 from jax.sharding import PartitionSpec as P
 
 EPSILON = 1e-05
+
+
+def gather_by_bits(value, axis, dim):
+    ways, here, step = (lax.axis_size(axis), lax.axis_index(axis), value.shape[dim])
+    line, have = (value, 1)
+    while have < ways:
+        line = jnp.concatenate(
+            [line, lax.ppermute(line, axis, [(d, (d - have) % ways) for d in range(ways)])],
+            axis=dim,
+        )
+        have = 2 * have
+    return jnp.roll(line, here * step, axis=dim)
 
 
 def layer_norm(values, gain):
@@ -129,7 +141,7 @@
     ).astype(jnp.float32)
     residual_rows = dealt_rows.astype(jnp.float32) + attn_rows
     normed_rows = layer_norm(residual_rows, mlp_gain).astype(jnp.bfloat16)
-    normed_all = lax.all_gather(normed_rows, "head", axis=2, tiled=True)
+    normed_all = gather_by_bits(normed_rows, "head", 2)
     inner = jax.nn.gelu(
         jnp.dot(
             normed_all.reshape(group_size * stretch_max, features),

time: 429 us -> 448 us (1.044)
  starting transfers between devices: 26.6 us -> 35.5 us
  local copies, waits for them, and re-layouts: 63.7 us -> 72.3 us
    all_gather x1 -> x0, waiting for transfers between devices: 73.6 us -> none  [local(): normed_all = lax.all_gather(normed_rows, 'head', axis=2, tiled=True)]
    ppermute x0 -> x3, waiting for transfers between devices: none -> 71.2 us  [gather_by_bits(): lax.ppermute(line, axis, [(d, (d - have) % ways) for d in range(ways)])]
    unnamed x44 -> x54, local copies, waits for them, and re-layouts: 21.7 us -> 27.9 us
    ppermute x0 -> x3, starting transfers between devices: none -> 4.98 us  [gather_by_bits(): lax.ppermute(line, axis, [(d, (d - have) % ways) for d in range(ways)])]
    unnamed x6 -> x5, waiting for transfers between devices: 125 us -> 128 us
  transfers between devices with their start and end apart: 10 -> 12, of which waited for: 5 -> 7; matrix products, arithmetic and copies ran while one was open for 18% -> 19% of each run, Pallas kernels for 0% -> 0%
where the time goes in v1:
time: 448 us; the launch traced here: 447 us
  waiting for transfers between devices  276 us (62%)
  local copies, waits for them, and re-layouts  72.3 us (16%)
  starting transfers between devices  35.5 us (8%)
  matrix products  25.6 us (6%)
  other arithmetic  23.6 us (5%)
  between operations  14.2 us (3%)
    unnamed x5, waiting for transfers between devices  128 us
    ppermute x3, waiting for transfers between devices, gather_by_bits(): lax.ppermute(line, axis, [(d, (d - have) % ways) for d in range(ways)])  71.2 us
    all_to_all x2, waiting for transfers between devices, local(): lax.all_to_all(dealt_cache, 'head', split_axis=3, concat_axis=2, tiled=True)  57.4 us
    unnamed x54, local copies, waits for them, and re-layouts  27.9 us
    all_to_all x2, waiting for transfers between devices, local(): lax.all_to_all(lax.all_to_all(dealt_cache, 'head', split_axis=3, concat_a...  18.9 us
    all_to_all x2, starting transfers between devices, local(): lax.all_to_all(dealt_cache, 'head', split_axis=3, concat_axis=2, tiled=True)  14.3 us
    dot_general x1, matrix products, local(): jnp.dot(inner, down_weight, preferred_element_type=jnp.float32)  14.3 us
  transfers between devices with their start and end apart: 12, of which 7 were waited for; matrix products, arithmetic and copies ran while one was open for 19% of the time, Pallas kernels for 0%

profile of v1, /device:TPU:0, one launch (start us, length us, event | category | flops | bytes accessed | tf_op | source)
XLA Modules:
  0.0 446.8 jit_solution(551083122537176693)
XLA Ops:
  8.0 1.4 gather_fusion
  10.1 1.5 gather_fusion.2
  12.4 4.2 all-to-all-start
  16.6 5.2 %slice_bitcast_fusion = (bf16[8,32,32,128]{3,2,1,0:T(8,128)(2,1)}, bf16[8,32,32,128]{3,2,1,0:T(8,128)(2,1)}) fusion(bf16[2,8,32,32,128]{4,3,2,1,0:T(8,128)(2,1)} %param.19), kind=kLoop, calls=%fused_computation.31 | loop fusion | bytes 8388608 | tf_op jit(solution)/shard_map/jit(_take)/Arg_0.9 | solution.py:96
  21.8 3.7 gather_fusion.6
  25.5 3.7 gather_fusion.3
  29.3 3.5 fusion.12
  32.8 2.1 copy.51
  35.7 6.5 %all-to-all-start.1 = ((bf16[1,8,32,32,128]{4,2,1,0,3:T(8,128)(2,1)}), bf16[1,8,32,32,128]{4,2,1,0,3:T(8,128)(2,1)}, u32[]{:S(2)}, u32[]{:S(2)}) async-start(bf16[1,8,32,32,128]{4,2,1,0,3:T(8,128)(2,1)} %copy.51), calls=%async_computation.1 | async-start | bytes 4194304 | tf_op jit(solution)/shard_map/all_to_all | solution.py:101
  45.7 1.3 iota_compare_fusion.1
  51.5 57.4 %all-to-all-done.1 = bf16[1,8,32,32,128]{4,2,1,0,3:T(8,128)(2,1)} async-done(((bf16[1,8,32,32,128]{4,2,1,0,3:T(8,128)(2,1)}), bf16[1,8,32,32,128]{4,2,1,0,3:T(8,128)(2,1)}, u32[]{:S(2)}, u32[]{:S(2)}) %all-to-all-start.1) | async-done | bytes 2097184 | tf_op jit(solution)/shard_map/all_to_all | solution.py:101
  108.9 2.0 copy.52
  110.9 1.9 copy.53
  112.8 4.4 all-to-all-start.2
  117.5 2.1 convert_reduce_fusion
  121.3 1.8 fusion.21
  124.1 18.9 %all-to-all-done.2 = bf16[1,8,256,4,128]{4,2,3,0,1:T(8,128)(2,1)} async-done(((bf16[1,8,256,4,128]{4,2,3,0,1:T(8,128)(2,1)}), bf16[1,8,256,4,128]{4,2,3,0,1:T(8,128)(2,1)}, u32[]{:S(2)}, u32[]{:S(2)}) %all-to-all-start.2) | async-done | bytes 2097184 | tf_op jit(solution)/shard_map/all_to_all | solution.py:100
  143.0 2.9 copy.55
  146.6 2.2 fusion.122
  148.8 2.3 convolution_convert_fusion.3
  151.1 2.0 fusion.121
  153.1 2.4 convolution_convert_fusion.2
  156.4 2.9 copy.83
  159.3 4.4 reshape.468
  164.4 65.8 %reduce-scatter.7.cloned.1.call-done = bf16[8,16384]{1,0:T(8,128)(2,1)} async-done(((bf16[64,16384]{1,0:T(8,128)(2,1)}), bf16[8,16384]{1,0:T(8,128)(2,1)}) %reduce-scatter.7.cloned.1.call-update) | async-done | bytes 262160
  230.3 1.1 reshape.469
  233.0 2.0 collective-permute-start
  235.0 5.1 %collective-permute-done = bf16[2,4,8,2048]{3,2,0,1:T(8,128)(2,1)S(1)} collective-permute-done((bf16[2,4,8,2048]{3,2,0,1:T(8,128)(2,1)S(1)}, bf16[2,4,8,2048]{3,2,0,1:T(8,128)(2,1)S(1)}, u32[]{:S(2)}, u32[]{:S(2)}) %collective-permute-start) | collective-permute-done | bytes 262176 | tf_op jit(solution)/shard_map/ppermute | solution.py:15
  240.2 1.7 collective-permute-start.1
  241.9 9.8 %collective-permute-done.1 = bf16[2,4,16,2048]{3,2,0,1:T(8,128)(2,1)S(1)} collective-permute-done((bf16[2,4,16,2048]{3,2,0,1:T(8,128)(2,1)S(1)}, bf16[2,4,16,2048]{3,2,0,1:T(8,128)(2,1)S(1)}, u32[]{:S(2)}, u32[]{:S(2)}) %collective-permute-start.1) | collective-permute-done | bytes 524320 | tf_op jit(solution)/shard_map/ppermute | solution.py:15
  252.8 1.2 collective-permute-start.2
  254.1 2.1 copy.61
  256.2 7.8 %all-to-all-start.4 = ((bf16[1,8,32,32,128]{4,2,1,0,3:T(8,128)(2,1)}), bf16[1,8,32,32,128]{4,2,1,0,3:T(8,128)(2,1)S(1)}, u32[]{:S(2)}, u32[]{:S(2)}) async-start(bf16[1,8,32,32,128]{4,2,1,0,3:T(8,128)(2,1)} %copy.61), calls=%async_computation.4 | async-start | bytes 4194304 | tf_op jit(solution)/shard_map/all_to_all | solution.py:101
  265.6 56.2 %collective-permute-done.2 = bf16[2,4,32,2048]{3,2,0,1:T(8,128)(2,1)} collective-permute-done((bf16[2,4,32,2048]{3,2,0,1:T(8,128)(2,1)}, bf16[2,4,32,2048]{3,2,0,1:T(8,128)(2,1)}, u32[]{:S(2)}, u32[]{:S(2)}) %collective-permute-start.2) | collective-permute-done | bytes 1048608 | tf_op jit(solution)/shard_map/ppermute | solution.py:15
  321.8 2.3 constant_dynamic-update-slice_fusion.4
  326.4 2.3 constant_dynamic-update-slice_fusion
  328.7 1.7 constant_dynamic-slice_fusion
  330.5 1.5 copy.59
  331.9 14.3 %convolution_convert_fusion = bf16[512,2048]{1,0:T(8,128)(2,1)} fusion(bf16[1024,2048]{1,0:T(8,128)(2,1)} %param.29, bf16[512,2048]{1,0:T(8,128)(2,1)} %bitcast.135, bf16[2048,1024]{1,0:T(8,128)(2,1)} %param.28), kind=kOutput, calls=%fused_computation.20 | convolution fusion | flops 4330094592 | bytes 12582912 | tf_op jit(solution)/shard_map/dot_general | solution.py:153
  346.2 4.5 %copy.82 = bf16[2,4,64,2048]{3,1,0,2:T(4,128)(2,1)} copy(bf16[2,4,64,2048]{3,2,1,0:T(8,128)(2,1)} %bitcast.136) | data formatting | bytes 4194304
  350.7 4.4 reshape.470
  356.6 1.9 copy.63
  358.5 3.9 all-to-all-start.5
  362.6 61.6 %reduce-scatter.9.cloned.1.call-done = bf16[8,16384]{1,0:T(8,128)(2,1)} async-done(((bf16[64,16384]{1,0:T(8,128)(2,1)}), bf16[8,16384]{1,0:T(8,128)(2,1)}) %reduce-scatter.9.cloned.1.call-update) | async-done | bytes 262160
  426.4 3.4 all-to-all-start.3
  429.8 2.0 pad_maximum_fusion
  431.8 5.5 %copy.65 = bf16[4,2,2,256,4,128]{5,4,3,2,1,0:T(4,128)(2,1)} copy(bf16[4,2,2,256,4,128]{5,3,4,2,0,1:T(8,128)(2,1)S(1)} %pad_maximum_fusion) | data formatting | bytes 8388608 | tf_op jit(solution)/shard_map/stack | solution.py:109
  438.0 1.5 gather_fusion.5
  (110 shorter events, 28.0 us)
Async XLA Ops:
  7.2 114.1 %copy-start = (bf16[2048,4,192]{0,2,1:T(8,128)(2,1)S(1)}, bf16[2048,4,192]{0,2,1:T(8,128)(2,1)}, u32[]{:S(2)}) copy-start(bf16[2048,4,192]{0,2,1:T(8,128)(2,1)} %param.24) | copy-start | bytes 9437188
  12.4 22.5 %all-to-all-start = ((bf16[8,8,2048]{2,1,0:T(8,128)(2,1)}), bf16[8,8,2048]{2,1,0:T(8,128)(2,1)S(1)}, u32[]{:S(2)}, u32[]{:S(2)}) async-start(bf16[8,8,2048]{2,1,0:T(8,128)(2,1)} %broadcast_select_fusion.1), calls=%async_computation | async-start | bytes 524288 | tf_op jit(solution)/shard_map/all_to_all | solution.py:111
  34.9 8.0 %copy-start.19 = (s32[8]{0:T(128)S(1)}, s32[8]{0:T(128)}, u32[]{:S(2)}) copy-start(s32[8]{0:T(128)} %param.22) | copy-start | bytes 100
  34.9 8.1 %copy-start.2 = (s32[8]{0:T(128)S(1)}, s32[8]{0:T(128)}, u32[]{:S(2)}) copy-start(s32[8]{0:T(128)} %param.21) | copy-start | bytes 100
  34.9 8.7 %copy-start.3 = (s32[8]{0:T(128)S(1)}, s32[8]{0:T(128)}, u32[]{:S(2)}) copy-start(s32[8]{0:T(128)} %param.20) | copy-start | bytes 100
  34.9 9.3 %copy-start.17 = (bf16[2048]{0:T(1024)(128)(2,1)S(1)}, bf16[2048]{0:T(1024)(128)(2,1)}, u32[]{:S(2)}) copy-start(bf16[2048]{0:T(1024)(128)(2,1)} %param.23) | copy-start | bytes 12292
  35.0 0.7 copy-start.5
  35.7 73.2 %all-to-all-start.1 = ((bf16[1,8,32,32,128]{4,2,1,0,3:T(8,128)(2,1)}), bf16[1,8,32,32,128]{4,2,1,0,3:T(8,128)(2,1)}, u32[]{:S(2)}, u32[]{:S(2)}) async-start(bf16[1,8,32,32,128]{4,2,1,0,3:T(8,128)(2,1)} %copy.51), calls=%async_computation.1 | async-start | bytes 4194304 | tf_op jit(solution)/shard_map/all_to_all | solution.py:101
  42.2 75.3 %all-gather.2.cloned.1.call-start = ((), (), s32[]{:S(2)}) async-start(), calls=%async_computation.8 | async-start | bytes 2359296 | tf_op jit(solution)/shard_map/all_gather | solution.py:114
  112.8 30.2 %all-to-all-start.2 = ((bf16[1,8,256,4,128]{4,2,3,0,1:T(8,128)(2,1)}), bf16[1,8,256,4,128]{4,2,3,0,1:T(8,128)(2,1)}, u32[]{:S(2)}, u32[]{:S(2)}) async-start(bf16[1,8,256,4,128]{4,2,3,0,1:T(8,128)(2,1)} %bitcast.122), calls=%async_computation.2 | async-start | bytes 4194304 | tf_op jit(solution)/shard_map/all_to_all | solution.py:100
  117.3 113.0 %reduce-scatter.7.cloned.1.call-start = ((), (), s32[]{:S(2)}) async-start(), calls=%async_computation.9 | async-start | bytes 2359296
  117.5 2.2 copy-start.4
  123.1 0.9 copy-start.14
  124.1 22.6 %copy-start.13 = (f32[256,512]{1,0:T(8,128)S(1)}, f32[256,512]{1,0:T(8,128)}, u32[]{:S(2)}) copy-start(f32[256,512]{1,0:T(8,128)} %subtract_convert_fusion.1) | copy-start | bytes 1572868
  124.1 22.6 %copy-start.20 = (f32[4]{0:T(128)S(1)}, f32[4]{0:T(128)}, u32[]{:S(2)}) copy-start(f32[4]{0:T(128)} %param.25) | copy-start | bytes 52
  146.6 4.5 %copy-start.15 = (bf16[256,4,128]{0,2,1:T(8,128)(2,1)}, bf16[256,4,128]{0,2,1:T(8,128)(2,1)S(1)}, u32[]{:S(2)}) copy-start(bf16[256,4,128]{0,2,1:T(8,128)(2,1)S(1)} %get-tuple-element.14) | copy-start | bytes 786436
  146.6 2.2 copy-start.16
  148.8 2.3 copy-start.12
  153.1 2.5 copy-start.11
  163.8 0.7 copy-start.18
  163.8 67.7 %copy-start.6 = (bf16[8,8,2048]{2,1,0:T(8,128)(2,1)S(1)}, bf16[8,8,2048]{2,1,0:T(8,128)(2,1)}, u32[]{:S(2)}) copy-start(bf16[8,8,2048]{2,1,0:T(8,128)(2,1)} %copy-done.5) | copy-start | bytes 786436
  232.1 22.0 %copy-start.7 = (bf16[1,8,32,32,128]{4,3,2,1,0:T(8,128)(2,1)S(1)}, bf16[1,8,32,32,128]{4,3,2,1,0:T(8,128)(2,1)}, u32[]{:S(2)}) copy-start(bf16[1,8,32,32,128]{4,3,2,1,0:T(8,128)(2,1)} %get-tuple-element.19) | copy-start | bytes 6291460
  233.0 18.7 %copy-start.8 = (bf16[2,4,8,2048]{3,2,0,1:T(8,128)(2,1)}, bf16[2,4,8,2048]{3,2,0,1:T(8,128)(2,1)S(1)}, u32[]{:S(2)}) copy-start(bf16[2,4,8,2048]{3,2,0,1:T(8,128)(2,1)S(1)} %get-tuple-element.8) | copy-start | bytes 786436
  233.0 7.1 %collective-permute-start = (bf16[2,4,8,2048]{3,2,0,1:T(8,128)(2,1)S(1)}, bf16[2,4,8,2048]{3,2,0,1:T(8,128)(2,1)S(1)}, u32[]{:S(2)}, u32[]{:S(2)}) collective-permute-start(bf16[2,4,8,2048]{3,2,0,1:T(8,128)(2,1)S(1)} %get-tuple-element.8), channel_id=1, source_target_pairs={{0,7},{1,0},{2,1},{3,2},{4,3},{5,4},{6,5},{7,6},{8,15},{9,8},{10,9... | collective-permute-start | bytes 786440 | tf_op jit(solution)/shard_map/ppermute | solution.py:15
  240.2 11.6 %collective-permute-start.1 = (bf16[2,4,16,2048]{3,2,0,1:T(8,128)(2,1)S(1)}, bf16[2,4,16,2048]{3,2,0,1:T(8,128)(2,1)S(1)}, u32[]{:S(2)}, u32[]{:S(2)}) collective-permute-start(bf16[2,4,16,2048]{3,2,0,1:T(8,128)(2,1)S(1)} %pad_maximum_fusion.2), channel_id=1, source_target_pairs={{0,6},{1,7},{2,0},{3,1},{4,2},{5,3},{6,4},{7,5},{8,14},{9,15},{10,... | collective-permute-start | bytes 1572872 | tf_op jit(solution)/shard_map/ppermute | solution.py:15
  252.8 69.0 %collective-permute-start.2 = (bf16[2,4,32,2048]{3,2,0,1:T(8,128)(2,1)}, bf16[2,4,32,2048]{3,2,0,1:T(8,128)(2,1)}, u32[]{:S(2)}, u32[]{:S(2)}) collective-permute-start(bf16[2,4,32,2048]{3,2,0,1:T(8,128)(2,1)} %pad_maximum_fusion.1), channel_id=1, source_target_pairs={{0,4},{1,5},{2,6},{3,7},{4,0},{5,1},{6,2},{7,3},{8,12},{9,13},{10,... | collective-permute-start | bytes 3145736 | tf_op jit(solution)/shard_map/ppermute | solution.py:15
  256.2 100.0 %all-to-all-start.4 = ((bf16[1,8,32,32,128]{4,2,1,0,3:T(8,128)(2,1)}), bf16[1,8,32,32,128]{4,2,1,0,3:T(8,128)(2,1)S(1)}, u32[]{:S(2)}, u32[]{:S(2)}) async-start(bf16[1,8,32,32,128]{4,2,1,0,3:T(8,128)(2,1)} %copy.61), calls=%async_computation.4 | async-start | bytes 4194304 | tf_op jit(solution)/shard_map/all_to_all | solution.py:101
  264.0 160.2 %reduce-scatter.9.cloned.1.call-start = ((), (), s32[]{:S(2)}) async-start(), calls=%async_computation.10 | async-start | bytes 2359296
  264.0 60.1 %copy-start.9 = (bf16[2,4,8,2048]{3,2,0,1:T(8,128)(2,1)S(1)}, bf16[2,4,8,2048]{3,2,0,1:T(8,128)(2,1)}, u32[]{:S(2)}) copy-start(bf16[2,4,8,2048]{3,2,0,1:T(8,128)(2,1)} %copy-done.8) | copy-start | bytes 786436
  358.5 67.8 %all-to-all-start.5 = ((bf16[1,8,256,4,128]{4,2,3,0,1:T(8,128)(2,1)}), bf16[1,8,256,4,128]{4,2,3,0,1:T(8,128)(2,1)S(1)}, u32[]{:S(2)}, u32[]{:S(2)}) async-start(bf16[1,8,256,4,128]{4,2,3,0,1:T(8,128)(2,1)} %bitcast.44), calls=%async_computation.5 | async-start | bytes 4194304 | tf_op jit(solution)/shard_map/all_to_all | solution.py:100
  426.4 10.9 %all-to-all-start.3 = ((bf16[2,4,8,2048]{3,2,0,1:T(8,128)(2,1)}), bf16[2,4,8,2048]{3,2,0,1:T(8,128)(2,1)S(1)}, u32[]{:S(2)}, u32[]{:S(2)}) async-start(bf16[2,4,8,2048]{3,2,0,1:T(8,128)(2,1)} %select_convert_fusion), calls=%async_computation.3 | async-start | bytes 524288 | tf_op jit(solution)/shard_map/all_to_all | solution.py:166
  431.7 8.5 %copy-start.1 = (bf16[2048,4,192]{0,2,1:T(8,128)(2,1)S(1)}, bf16[2048,4,192]{0,2,1:T(8,128)(2,1)}, u32[]{:S(2)}) copy-start(bf16[2048,4,192]{0,2,1:T(8,128)(2,1)} %param.24) | copy-start | bytes 9437188
  437.3 0.7 copy-start.10
Sparse Core Ops, SparseCore 0:
  45.8 71.0 all-gather.1
  163.9 66.3 reduce-scatter.6
  355.3 68.8 reduce-scatter.8
